TPU v7x, 512 devices: a whole 4x4x16 slice. The times are simulated.
512 devices in a mesh: row: 32 (over x, z_hi, core), col: 16 (over z_lo, y).
Axes of the slice: x: 4, y: 4, z: 16 (z_hi: 4, z_lo: 4; z = z_hi * 4 + z_lo), core: 2. Of those that a mesh axis runs over, the one named last changes fastest.
Arguments:
- images: bfloat16 [32, 128, 128, 256], P('row', 'col'), may hold values from -6 to 6
- weight: bfloat16 [3, 3, 256, 256], P(None, None, None, 'col'), may hold values from -0.125 to 0.125
- norm_gain: float32 [256], replicated, may hold values from 0.5 to 1.5
- cotangent: bfloat16 [32, 128, 128, 256], P('row', 'col'), may hold values from -6 to 6
Outputs:
- features: bfloat16 [32, 128, 128, 256], P('row', 'col')
- input_grad: bfloat16 [32, 128, 128, 256], P('row', 'col')
- weight_grad: float32 [3, 3, 256, 256], P(None, None, None, 'col')
All inputs are finite; a program needn't handle non-finite values.
Results may differ from a plain program's by a relative error of at most 0.013.
Values may be sent and summed in bfloat16 or wider, within the bound.
No kernel may reach another device: no remote copies, remote signals or barrier semaphores. Data moves between devices by JAX's collectives and lax.ppermute only.
A program may use at most 64 MiB of HBM per device.

v0:
```python
import math
import jax
import jax.numpy as jnp
from jax import lax
from jax.sharding import PartitionSpec as P

epsilon = 1e-06
root_half = 0.7071067811865476
norm_const = 0.3989422804014327


def padded_2(value, sides, width):
    for axis, dim in sides:
        peers, length = (lax.axis_size(axis), value.shape[dim])
        up = [(i, (i + 1) % peers) for i in range(peers - 1)]
        down = [(j, i) for i, j in up]
        last = lax.slice_in_dim(value, length - width, length, axis=dim)
        initial = lax.slice_in_dim(value, 0, width, axis=dim)
        before = lax.ppermute(last, axis, up)
        after = lax.ppermute(initial, axis, down)
        value = jnp.concatenate([before, value, after], axis=dim)
    return value


def norm_act(conv_out, upper, norm_gain):
    mean_val = jnp.mean(conv_out, axis=-1, keepdims=True)
    centred = conv_out - mean_val
    variance = jnp.mean(centred * centred, axis=-1, keepdims=True)
    inv_std = lax.rsqrt(variance + epsilon)
    unit = centred * inv_std
    normed = unit * norm_gain
    cdf_val = 0.5 * (1.0 + lax.erf(normed * root_half))
    density = jnp.exp(-0.5 * normed * normed) * norm_const
    outputs = (normed * cdf_val).astype(jnp.bfloat16)
    upstream = upper.astype(jnp.float32) * (cdf_val + normed * density) * norm_gain
    mean_up = jnp.mean(upstream, axis=-1, keepdims=True)
    mean_cross = jnp.mean(upstream * unit, axis=-1, keepdims=True)
    grad_pre = inv_std * (upstream - mean_up - unit * mean_cross)
    return (outputs, grad_pre.astype(jnp.bfloat16))


def window(padded, tap_row, tap_col, tile_rows, tile_cols):
    return padded[:, tap_row : tap_row + tile_rows, tap_col : tap_col + tile_cols, :].reshape(
        -1, padded.shape[-1]
    )


def on_device(images, weight, norm_gain, cotangent):
    img_count, tile_rows, tile_cols, in_chan = images.shape
    whole_kernel = lax.all_gather(weight, "col", axis=3, tiled=True)
    out_chan = whole_kernel.shape[3]
    rimmed = padded_2(images, (("col", 1),), 1)
    padded = jnp.pad(rimmed, ((0, 0), (0, 0), (1, 1), (0, 0)))
    conv_out = jnp.zeros((img_count * tile_rows * tile_cols, out_chan), jnp.float32)
    for tap_row in range(3):
        for tap_col in range(3):
            conv_out = conv_out + jnp.dot(
                window(padded, tap_row, tap_col, tile_rows, tile_cols),
                whole_kernel[tap_row, tap_col],
                preferred_element_type=jnp.float32,
            )
    outputs, grad_pre = norm_act(conv_out, cotangent.reshape(-1, out_chan), norm_gain)
    grad_grid = grad_pre.reshape(img_count, tile_rows, tile_cols, out_chan)
    grad_rimmed = padded_2(grad_grid, (("col", 1),), 1)
    grad_pad = jnp.pad(grad_rimmed, ((0, 0), (0, 0), (1, 1), (0, 0)))
    grad_input = jnp.zeros((img_count * tile_rows * tile_cols, in_chan), jnp.float32)
    pieces = []
    for tap_row in range(3):
        for tap_col in range(3):
            grad_input = grad_input + lax.dot_general(
                window(grad_pad, 2 - tap_row, 2 - tap_col, tile_rows, tile_cols),
                whole_kernel[tap_row, tap_col],
                (((1,), (1,)), ((), ())),
                preferred_element_type=jnp.float32,
            )
            pieces.append(
                lax.dot_general(
                    window(padded, tap_row, tap_col, tile_rows, tile_cols),
                    grad_pre,
                    (((0,), (0,)), ((), ())),
                    preferred_element_type=jnp.float32,
                )
            )
    partial_value = jnp.stack(pieces).reshape(3, 3, in_chan, out_chan)
    totals = lax.psum(partial_value, ("row", "col"))
    col_share = out_chan // lax.axis_size("col")
    own_share = lax.dynamic_slice_in_dim(totals, lax.axis_index("col") * col_share, col_share, 3)
    pixels = img_count * lax.axis_size("row") * tile_rows * lax.axis_size("col") * tile_cols
    weight_grad = own_share * (1.0 / math.sqrt(pixels))
    features = outputs.reshape(img_count, tile_rows, tile_cols, out_chan)
    input_grad = grad_input.astype(jnp.bfloat16).reshape(img_count, tile_rows, tile_cols, in_chan)
    return (features, input_grad, weight_grad)


def solution(mesh):
    placed = (
        P("row", "col", None, None),
        P(None, None, None, "col"),
        P(),
        P("row", "col", None, None),
    )
    return jax.shard_map(
        on_device,
        mesh=mesh,
        in_specs=placed,
        out_specs=(
            P("row", "col", None, None),
            P("row", "col", None, None),
            P(None, None, None, "col"),
        ),
        check_vma=False,
    )
```

profile of v0, /device:TPU:2, one launch (start us, length us, event | category | flops | bytes accessed | tf_op | source)
XLA Modules:
  0.0 616.7 jit_solution(12036107945683514388)
XLA Ops:
  7.2 0.7 all-gather.2.cloned.1.call-update
  8.0 0.9 fusion.29
  8.8 3.5 collective-permute-start
  12.3 1.3 collective-permute-start.1
  13.6 0.6 collective-permute-done
  14.2 4.3 collective-permute-done.1
  18.5 1.2 select_maximum_fusion.2
  19.7 1.0 pad_maximum_fusion.2
  20.8 1.4 fusion.27
  22.1 79.2 %all-gather.2.cloned.1.call-done = bf16[3,3,256,256]{2,3,1,0:T(8,128)(2,1)} async-done(((bf16[3,3,256,16]{2,3,1,0:T(8,128)(2,1)}), bf16[3,3,256,256]{2,3,1,0:T(8,128)(2,1)}) %all-gather.2.cloned.1.call-update) | async-done | bytes 1179664 | tf_op jit(solution)/shard_map/all_gather | solution.py:50
  101.3 1.4 fusion.21
  102.7 0.3 fusion.23
  103.0 0.3 convolution_add_fusion.13
  103.4 0.7 copy-done.6
  104.0 0.3 convolution_add_fusion.12
  104.4 0.3 convolution_add_fusion.11
  104.8 0.3 convolution_add_fusion.10
  105.1 0.7 copy-done.4
  105.8 0.3 convolution_add_fusion.9
  106.2 0.3 convolution_add_fusion.8
  106.5 0.7 copy-done.7
  107.2 0.4 fusion.30
  107.7 0.4 multiply_reduce_fusion.1
  108.1 0.6 copy-done.9
  108.7 1.9 fusion.24
  110.6 0.8 multiply_convert_fusion
  111.5 1.0 fusion.12
  112.5 1.1 fusion.11
  113.5 1.1 fusion.10
  114.6 1.1 fusion.9
  115.7 1.0 fusion.8
  116.7 1.0 fusion.7
  117.8 1.0 fusion.6
  118.8 1.0 fusion.5
  119.8 3.0 collective-permute-start.2
  122.9 1.3 collective-permute-start.3
  124.2 1.0 fusion.4
  125.2 3.1 copy.8
  128.4 0.6 collective-permute-done.3
  129.2 0.4 fusion.26
  129.7 0.3 fusion.20
  130.0 0.3 fusion.22
  130.3 0.3 convolution_add_fusion.6
  130.6 0.3 convolution_add_fusion.5
  131.5 0.3 convolution_add_fusion.2
  132.1 1.1 fusion.3
  133.2 475.1 %all-reduce.4.cloned.1.call-done = f32[3,3,256,256]{2,3,1,0:T(8,128)} async-done(((f32[3,3,256,256]{2,3,1,0:T(8,128)}), f32[3,3,256,256]{2,3,1,0:T(8,128)}) %all-reduce.4.cloned.1.call-update) | async-done | bytes 2359312 | tf_op jit(solution)/shard_map/psum | solution.py:85
  608.3 1.6 dynamic-slice_multiply_fusion
  (31 shorter events, 1.4 us)
Async XLA Ops:
  7.2 12.6 %copy-start = (bf16[1,8,128,256]{3,2,1,0:T(8,128)(2,1)S(1)}, bf16[1,8,128,256]{3,2,1,0:T(8,128)(2,1)}, u32[]{:S(2)}) copy-start(bf16[1,8,128,256]{3,2,1,0:T(8,128)(2,1)} %param.4) | copy-start | bytes 1572868
  7.2 94.1 %all-gather.2.cloned.1.call-start = ((), (), s32[]{:S(2)}) async-start(), calls=%async_computation | async-start | bytes 1253376 | tf_op jit(solution)/shard_map/all_gather | solution.py:50
  7.9 600.3 %all-reduce.4.cloned.1.call-start = ((), (), s32[]{:S(2)}) async-start(), calls=%async_computation.1 | async-start | bytes 4718592 | tf_op jit(solution)/shard_map/psum | solution.py:85
  8.8 5.4 collective-permute-start
  12.3 6.2 collective-permute-start.1
  22.1 84.1 %copy-start.2 = (bf16[1,8,128,256]{3,2,1,0:T(8,128)(2,1)}, bf16[1,8,128,256]{3,2,1,0:T(8,128)(2,1)S(1)}, u32[]{:S(2)}) copy-start(bf16[1,8,128,256]{3,2,1,0:T(8,128)(2,1)S(1)} %get-tuple-element.13) | copy-start | bytes 1572868
  101.3 1.4 copy-start.1
  101.3 1.7 copy-start.8
  103.0 1.0 copy-start.6
  103.4 1.1 copy-start.5
  104.8 1.0 copy-start.4
  106.2 1.0 copy-start.7
  107.2 0.8 copy-start.10
  107.6 1.0 copy-start.9
  115.7 2.1 copy-start.3
  119.8 8.6 %collective-permute-start.2 = (bf16[1,1,128,256]{3,2,1,0:T(8,128)(2,1)S(1)}, bf16[1,1,128,256]{3,2,1,0:T(8,128)(2,1)S(1)}, u32[]{:S(2)}, u32[]{:S(2)}) collective-permute-start(bf16[1,1,128,256]{3,2,1,0:T(8,128)(2,1)S(1)} %get-tuple-element.21), channel_id=1, source_target_pairs={{0,1},{1,2},{2,3},{3,4},{4,5},{5,6},{6,7},{7,8},{8,9},{9,10},{10,1... | collective-permute-start | bytes 196616 | tf_op jit(solution)/shard_map/ppermute | solution.py:19
  122.9 6.2 collective-permute-start.3
Sparse Core Ops, SparseCore 0:
  10.1 91.1 all-gather.1
  128.5 479.7 all-reduce.3
where the time goes:
time: 617 us
  waiting for transfers between devices  560 us (91%)
  matrix products  17 us (3%)
  between operations  14.3 us (2%)
  starting transfers between devices  9.17 us (1%)
  local copies, waits for them, and re-layouts  8.58 us (1%)
  other arithmetic  7.21 us (1%)
    psum x1, waiting for transfers between devices, on_device(): totals = lax.psum(partial_value, ('row', 'col'))  475 us
    all_gather x1, waiting for transfers between devices, on_device(): whole_kernel = lax.all_gather(weight, 'col', axis=3, tiled=True)  79.2 us
  transfers between devices with their start and end apart: 6, of which 5 were waited for; matrix products, arithmetic and copies ran while one was open for 2% of the time, Pallas kernels for 0%

commit v1 on v0

--- a/solution.py
+++ b/solution.py
@@ -82,7 +82,13 @@
                 )
             )
     partial_value = jnp.stack(pieces).reshape(3, 3, in_chan, out_chan)
-    totals = lax.psum(partial_value, ("row", "col"))
+
+    def wait_ports(obj):
+        for dev in ("col", "row"):
+            obj = lax.psum(obj, dev)
+        return obj
+
+    totals = wait_ports(partial_value)
     col_share = out_chan // lax.axis_size("col")
     own_share = lax.dynamic_slice_in_dim(totals, lax.axis_index("col") * col_share, col_share, 3)
     pixels = img_count * lax.axis_size("row") * tile_rows * lax.axis_size("col") * tile_cols

time: 617 us -> 669 us (1.084)
  the two profiles are of different devices: /device:TPU:2 before, /device:TPU:1 now
where the time goes in v1:
time: 669 us; the launch traced here: 668 us
  waiting for transfers between devices  609 us (91%)
  matrix products  16.9 us (3%)
  between operations  14.1 us (2%)
  local copies, waits for them, and re-layouts  11.2 us (2%)
  starting transfers between devices  9.45 us (1%)
  other arithmetic  7.23 us (1%)
    psum x2, waiting for transfers between devices, wait_ports(): obj = lax.psum(obj, dev)  531 us
    all_gather x1, waiting for transfers between devices, on_device(): whole_kernel = lax.all_gather(weight, 'col', axis=3, tiled=True)  70.6 us
  transfers between devices with their start and end apart: 7, of which 5 were waited for; matrix products, arithmetic and copies ran while one was open for 1% of the time, Pallas kernels for 0%

profile of v1, /device:TPU:1, one launch (start us, length us, event | category | flops | bytes accessed | tf_op | source)
XLA Modules:
  0.0 668.3 jit_solution(7160664566902318417)
XLA Ops:
  7.2 0.7 all-gather.2.cloned.1.call-update
  8.0 0.9 fusion.29
  8.8 4.0 collective-permute-start
  12.9 1.3 collective-permute-start.1
  14.2 3.7 collective-permute-done.1
  17.9 1.2 select_maximum_fusion.2
  19.1 1.0 pad_maximum_fusion.2
  20.2 1.4 fusion.27
  21.5 70.6 %all-gather.2.cloned.1.call-done = bf16[3,3,256,256]{2,3,1,0:T(8,128)(2,1)} async-done(((bf16[3,3,256,16]{2,3,1,0:T(8,128)(2,1)}), bf16[3,3,256,256]{2,3,1,0:T(8,128)(2,1)}) %all-gather.2.cloned.1.call-update) | async-done | bytes 1179664 | tf_op jit(solution)/shard_map/all_gather | solution.py:50
  92.2 1.4 fusion.21
  93.5 0.3 fusion.23
  93.9 0.3 convolution_add_fusion.13
  94.3 0.7 copy-done.6
  94.9 0.3 convolution_add_fusion.12
  95.3 0.3 convolution_add_fusion.11
  95.7 0.3 convolution_add_fusion.10
  96.0 0.7 copy-done.4
  96.7 0.3 convolution_add_fusion.9
  97.1 0.3 convolution_add_fusion.8
  97.4 0.7 copy-done.11
  98.1 0.4 fusion.30
  98.5 0.4 multiply_reduce_fusion.1
  98.9 0.6 copy-done.13
  99.6 1.9 fusion.24
  101.5 0.8 multiply_convert_fusion
  102.3 1.0 fusion.12
  103.4 1.0 fusion.11
  104.4 1.0 fusion.10
  105.4 1.0 fusion.9
  106.5 1.1 fusion.8
  107.5 1.0 fusion.7
  108.6 1.0 fusion.6
  109.6 1.1 fusion.5
  110.7 1.0 fusion.4
  111.7 3.0 copy.8
  114.8 2.7 collective-permute-start.2
  117.6 1.3 collective-permute-start.3
  118.9 3.7 collective-permute-done.3
  122.8 1.6 fusion.26
  124.6 167.9 %all-reduce.5.cloned.1.call-done = f32[3,3,256,256]{2,3,1,0:T(8,128)} async-done(((f32[3,3,256,256]{2,3,1,0:T(8,128)}), f32[3,3,256,256]{2,3,1,0:T(8,128)}) %all-reduce.5.cloned.1.call-update) | async-done | bytes 2359312 | tf_op jit(solution)/shard_map/psum | solution.py:88
  292.9 0.3 convolution_add_fusion.6
  293.2 0.7 copy-done.10
  293.9 0.3 convolution_add_fusion.5
  294.9 0.7 copy-done.8
  295.6 0.3 convolution_add_fusion.2
  296.3 1.1 fusion.3
  297.4 362.8 %all-reduce.7.cloned.1.call-done = f32[3,3,256,256]{2,3,1,0:T(8,128)} async-done(((f32[3,3,256,256]{2,3,1,0:T(8,128)}), f32[3,3,256,256]{2,3,1,0:T(8,128)}) %all-reduce.7.cloned.1.call-update) | async-done | bytes 2359312 | tf_op jit(solution)/shard_map/psum | solution.py:88
  660.2 1.6 dynamic-slice_multiply_fusion
  (42 shorter events, 2.1 us)
Async XLA Ops:
  7.2 12.0 %copy-start = (bf16[1,8,128,256]{3,2,1,0:T(8,128)(2,1)S(1)}, bf16[1,8,128,256]{3,2,1,0:T(8,128)(2,1)}, u32[]{:S(2)}) copy-start(bf16[1,8,128,256]{3,2,1,0:T(8,128)(2,1)} %param.4) | copy-start | bytes 1572868
  7.2 85.0 %all-gather.2.cloned.1.call-start = ((), (), s32[]{:S(2)}) async-start(), calls=%async_computation | async-start | bytes 1253376 | tf_op jit(solution)/shard_map/all_gather | solution.py:50
  7.9 284.6 %all-reduce.5.cloned.1.call-start = ((), (), s32[]{:S(2)}) async-start(), calls=%async_computation.1 | async-start | bytes 4718592 | tf_op jit(solution)/shard_map/psum | solution.py:88
  8.8 5.4 collective-permute-start
  12.9 5.0 collective-permute-start.1
  21.5 75.5 %copy-start.2 = (bf16[1,8,128,256]{3,2,1,0:T(8,128)(2,1)}, bf16[1,8,128,256]{3,2,1,0:T(8,128)(2,1)S(1)}, u32[]{:S(2)}) copy-start(bf16[1,8,128,256]{3,2,1,0:T(8,128)(2,1)S(1)} %get-tuple-element.13) | copy-start | bytes 1572868
  92.2 1.4 copy-start.1
  92.2 1.7 copy-start.12
  93.9 1.0 copy-start.6
  94.2 1.1 copy-start.5
  95.7 1.0 copy-start.4
  97.0 1.0 copy-start.11
  98.1 0.8 copy-start.14
  98.5 1.0 copy-start.13
  106.5 2.1 copy-start.3
  114.8 545.4 %all-reduce.7.cloned.1.call-start = ((), (), s32[]{:S(2)}) async-start(), calls=%async_computation.2 | async-start | bytes 4718592 | tf_op jit(solution)/shard_map/psum | solution.py:88
  114.8 4.0 collective-permute-start.2
  117.6 5.0 collective-permute-start.3
  292.9 1.0 copy-start.10
  293.2 1.1 copy-start.9
  294.6 1.0 copy-start.8
  294.9 1.1 copy-start.7
Sparse Core Ops, SparseCore 0:
  10.1 82.0 all-gather.1
  114.9 177.5 all-reduce.4
  295.4 364.6 all-reduce.6
